TPU v7x, 32 devices: a whole 2x2x4 slice. The times are simulated.
32 devices in a mesh: band: 8 (over y, x, core), date: 4 (over z).
Axes of the slice: x: 2, y: 2, z: 4, core: 2. Of those that a mesh axis runs over, the one named last changes fastest.
Arguments:
- inputs: bfloat16 [8, 32, 128, 512], P('date', 'band'), may hold values from -6 to 6
- preact_one: bfloat16 [8, 32, 128, 512], P('date', 'band'), may hold values from -8 to 8
- preact_two: bfloat16 [8, 32, 128, 512], P('date', 'band'), may hold values from -8 to 8
- cotangent: bfloat16 [8, 32, 128, 512], P('date', 'band'), may hold values from -6 to 6
- weight_one: bfloat16 [3, 3, 512, 512], replicated, may hold values from -0.09375 to 0.09375
- weight_two: bfloat16 [3, 3, 512, 512], replicated, may hold values from -0.09375 to 0.09375
Outputs:
- input_grad: bfloat16 [8, 32, 128, 512], P('date', 'band')
- weight_grad_one: float32 [4608, 512], P('date')
- weight_grad_two: float32 [4608, 512], P('date')
All inputs are finite; a program needn't handle non-finite values.
Results may differ from a plain program's by a relative error of at most 0.0057.
Values may be sent and summed in bfloat16 or wider, within the bound.
No kernel may reach another device: no remote copies, remote signals or barrier semaphores. Data moves between devices by JAX's collectives and lax.ppermute only.
A program may use at most 128 MiB of HBM per device.

v0:
```python
import jax
import jax.numpy as jnp
from jax import lax
from jax.sharding import PartitionSpec as P


def extended(array, sides, width):
    for axis, dim in sides:
        peers, length = (lax.axis_size(axis), array.shape[dim])
        up = [(i, (i + 1) % peers) for i in range(peers - 1)]
        down = [(j, i) for i, j in up]
        last = lax.slice_in_dim(array, length - width, length, axis=dim)
        leading = lax.slice_in_dim(array, 0, width, axis=dim)
        before = lax.ppermute(last, axis, up)
        after = lax.ppermute(leading, axis, down)
        array = jnp.concatenate([before, array, after], axis=dim)
    return array


def slope(field_value):
    logistic = jax.nn.sigmoid(field_value)
    return logistic * (1.0 + field_value * (1.0 - logistic))


def pad_columns(field_value):
    return jnp.pad(field_value, ((0, 0), (0, 0), (1, 1), (0, 0)))


def shifted(padded, row_offset, col_offset, row_count, rim_start):
    col_count = padded.shape[2] - 2
    return padded[
        :,
        rim_start - row_offset : rim_start - row_offset + row_count,
        1 - col_offset : 1 - col_offset + col_count,
        :,
    ]


def weight_terms(left_field, padded, rim_start, grad_scale):
    row_count = left_field.shape[1]
    tap_list = []
    for row_offset in (-1, 0, 1):
        for col_offset in (-1, 0, 1):
            shifted_piece = shifted(padded, row_offset, col_offset, row_count, rim_start)
            tap_list.append(
                lax.dot_general(
                    left_field,
                    shifted_piece,
                    (((0, 1, 2), (0, 1, 2)), ((), ())),
                    preferred_element_type=jnp.float32,
                )
            )
    stacked = jnp.stack(tap_list)
    return (stacked * grad_scale).reshape(-1, stacked.shape[2])


def back_terms(padded, weight, row_count, rim_start):
    accumulated = None
    for row_offset in (-1, 0, 1):
        for col_offset in (-1, 0, 1):
            shifted_piece = shifted(padded, row_offset, col_offset, row_count, rim_start)
            product = lax.dot_general(
                shifted_piece,
                weight[row_offset + 1, col_offset + 1],
                (((3,), (1,)), ((), ())),
                preferred_element_type=jnp.float32,
            )
            accumulated = product if accumulated is None else accumulated + product
    return accumulated


def settle(grad_term):
    dates, bands = (lax.axis_size("date"), lax.axis_size("band"))
    rows, cols = grad_term.shape
    piece = rows // (dates * bands)
    by_band = grad_term.reshape(dates, bands, piece, cols).swapaxes(0, 1).reshape(rows, cols)
    share = lax.psum_scatter(by_band, "band", scatter_dimension=0, tiled=True)
    share = lax.psum_scatter(share, "date", scatter_dimension=0, tiled=True)
    return lax.all_gather(share, "band", axis=0, tiled=True)


def body(inputs, preact_one, preact_two, cotangent, weight_one, weight_two):
    row_count = inputs.shape[1]
    grad_scale = 1.0 / (inputs.shape[0] * lax.axis_size("date"))
    act_one = jax.nn.silu(preact_one.astype(jnp.float32)).astype(jnp.bfloat16)
    delta_two = (cotangent.astype(jnp.float32) * slope(preact_two.astype(jnp.float32))).astype(
        jnp.bfloat16
    )
    padded_two = pad_columns(extended(delta_two, (("band", 1),), 1))
    term_two = weight_terms(act_one, padded_two, 1, grad_scale)
    grad_two = settle(term_two)
    back_one = back_terms(padded_two, weight_two, row_count, 1)
    delta_one = (back_one * slope(preact_one.astype(jnp.float32))).astype(jnp.bfloat16)
    padded_one = pad_columns(extended(delta_one, (("band", 1),), 1))
    term_one = weight_terms(inputs, padded_one, 1, grad_scale)
    grad_one = settle(term_one)
    input_grad = back_terms(padded_one, weight_one, row_count, 1).astype(jnp.bfloat16)
    return (input_grad, grad_one, grad_two)


def solution(mesh):
    placed = (
        P("date", "band", None, None),
        P("date", "band", None, None),
        P("date", "band", None, None),
        P("date", "band", None, None),
        P(),
        P(),
    )
    return jax.shard_map(
        body,
        mesh=mesh,
        in_specs=placed,
        out_specs=(P("date", "band", None, None), P("date", None), P("date", None)),
        check_vma=False,
    )
```

profile of v0, /device:TPU:0, one launch (start us, length us, event | category | flops | bytes accessed | tf_op | source)
XLA Modules:
  0.0 340.1 jit_solution(716486030727833753)
XLA Ops:
  7.2 0.0 reduce-scatter.9.cloned.1.call-start
  7.2 2.5 fusion.7
  9.8 1.4 collective-permute-start.1
  11.2 3.0 collective-permute-start
  14.3 1.1 collective-permute-done
  15.4 0.4 fusion.20
  15.8 2.0 fusion.31
  17.9 1.7 fusion.30
  19.6 1.8 fusion.29
  21.4 2.0 fusion.28
  23.4 1.8 fusion.27
  25.2 1.8 fusion.26
  26.9 2.0 fusion.25
  28.9 1.9 fusion.24
  30.8 1.8 fusion.23
  32.6 4.8 %broadcast_multiply_fusion = f32[9,512,512]{2,1,0:T(8,128)S(1)} fusion(f32[9,512,512]{2,1,0:T(8,128)} %fusion.23), kind=kLoop, calls=%fused_computation.2 | loop fusion | flops 2359296 | bytes 18874368 | tf_op jit(solution)/shard_map/mul | solution.py:54
  37.5 4.8 %copy.28 = f32[8,4,144,512]{3,2,1,0:T(8,128)} copy(f32[8,4,144,512]{3,2,0,1:T(8,128)S(1)} %bitcast.311) | data formatting | bytes 18874368 | tf_op jit(solution)/shard_map/transpose | solution.py:76
  42.3 0.2 reduce-scatter.5.cloned.1.call-start
  42.5 2.2 fusion.109
  44.8 1.8 fusion.43
  46.7 1.8 fusion.39
  48.5 0.7 fusion.79
  49.2 0.7 fusion.82
  50.0 0.7 fusion.85
  50.7 0.7 fusion.88
  51.5 0.7 fusion.91
  52.2 0.5 copy-done.7
  52.7 1.7 fusion.14
  54.5 1.3 collective-permute-start.3
  55.8 7.3 %collective-permute-start.2 = (bf16[2,1,128,512]{3,2,1,0:T(8,128)(2,1)S(1)}, bf16[2,1,128,512]{3,2,1,0:T(8,128)(2,1)S(1)}, u32[]{:S(2)}, u32[]{:S(2)}) collective-permute-start(bf16[2,1,128,512]{3,2,1,0:T(8,128)(2,1)S(1)} %get-tuple-element.4), channel_id=1, source_target_pairs={{0,4},{4,8},{8,12},{12,16},{16,20},{20,24},{24,28},{1,5},{5,9},{9,... | collective-permute-start | bytes 786440 | tf_op jit(solution)/shard_map/ppermute | solution.py:14
  63.1 1.5 collective-permute-done.2
  64.5 0.4 select_maximum_fusion
  65.0 1.8 fusion.38
  66.8 1.7 fusion.22
  68.5 1.8 fusion.37
  70.2 1.8 fusion.36
  72.0 1.7 fusion.35
  73.7 1.8 fusion.34
  75.5 1.7 fusion.33
  77.3 1.8 fusion.21
  79.0 1.7 fusion.32
  80.7 5.2 %broadcast_multiply_fusion.1 = f32[9,512,512]{2,1,0:T(8,128)S(1)} fusion(f32[9,512,512]{2,1,0:T(8,128)} %fusion.32), kind=kLoop, calls=%fused_computation.3 | loop fusion | flops 2359296 | bytes 18874368 | tf_op jit(solution)/shard_map/mul | solution.py:54
  85.9 4.7 %copy.18 = f32[8,4,144,512]{3,2,1,0:T(8,128)} copy(f32[8,4,144,512]{3,2,0,1:T(8,128)S(1)} %bitcast.312) | data formatting | bytes 18874368 | tf_op jit(solution)/shard_map/transpose | solution.py:76
  90.7 0.0 reduce-scatter.11.cloned.1.call-start
  90.7 35.9 %reduce-scatter.9.cloned.1.call-done = f32[576,512]{1,0:T(8,128)} async-done(((f32[4608,512]{1,0:T(8,128)}), f32[576,512]{1,0:T(8,128)}) %reduce-scatter.9.cloned.1.call-update) | async-done | bytes 1179664 | tf_op jit(solution)/shard_map/reduce_scatter | solution.py:77
  126.6 0.0 reduce-scatter.7.cloned.1.call-start
  126.7 80.0 %reduce-scatter.5.cloned.1.call-done = f32[576,512]{1,0:T(8,128)} async-done(((f32[4608,512]{1,0:T(8,128)}), f32[576,512]{1,0:T(8,128)}) %reduce-scatter.5.cloned.1.call-update) | async-done | bytes 1179664 | tf_op jit(solution)/shard_map/reduce_scatter | solution.py:77
  206.7 0.0 all-gather.5.cloned.1.call-start
  206.7 31.5 %reduce-scatter.11.cloned.1.call-done = f32[144,512]{1,0:T(8,128)} async-done(((f32[576,512]{1,0:T(8,128)}), f32[144,512]{1,0:T(8,128)}) %reduce-scatter.11.cloned.1.call-update) | async-done | bytes 294928 | tf_op jit(solution)/shard_map/reduce_scatter | solution.py:78
  238.2 0.3 all-gather.3.cloned.1.call-start
  238.5 29.8 %reduce-scatter.7.cloned.1.call-done = f32[144,512]{1,0:T(8,128)} async-done(((f32[576,512]{1,0:T(8,128)}), f32[144,512]{1,0:T(8,128)}) %reduce-scatter.7.cloned.1.call-update) | async-done | bytes 294928 | tf_op jit(solution)/shard_map/reduce_scatter | solution.py:78
  268.3 2.2 fusion.99
  270.6 1.8 fusion.93
  272.4 1.8 fusion.94
  274.3 0.7 fusion.59
  275.0 0.7 fusion.62
  275.8 0.7 fusion.65
  276.5 0.7 fusion.68
  277.3 0.7 fusion.71
  278.0 2.2 add_convert_fusion
  280.2 17.6 %all-gather.5.cloned.1.call-done = f32[1152,512]{1,0:T(8,128)} async-done(((f32[144,512]{1,0:T(8,128)}), f32[1152,512]{1,0:T(8,128)}) %all-gather.5.cloned.1.call-update) | async-done | bytes 2359312 | tf_op jit(solution)/shard_map/all_gather | solution.py:79
  297.8 30.8 %all-gather.3.cloned.1.call-done = f32[1152,512]{1,0:T(8,128)} async-done(((f32[144,512]{1,0:T(8,128)}), f32[1152,512]{1,0:T(8,128)}) %all-gather.3.cloned.1.call-update) | async-done | bytes 2359312 | tf_op jit(solution)/shard_map/all_gather | solution.py:79
  328.6 3.3 copy.101
  331.8 1.4 copy.102
  (35 shorter events, 0.3 us)
Async XLA Ops:
  7.2 57.8 %copy-start = (bf16[2,4,128,512]{3,2,1,0:T(8,128)(2,1)S(1)}, bf16[2,4,128,512]{3,2,1,0:T(8,128)(2,1)}, u32[]{:S(2)}) copy-start(bf16[2,4,128,512]{3,2,1,0:T(8,128)(2,1)} %param.6) | copy-start | bytes 3145732
  7.2 119.4 %reduce-scatter.9.cloned.1.call-start = ((), (), s32[]{:S(2)}) async-start(), calls=%async_computation.7 | async-start | bytes 10616832 | tf_op jit(solution)/shard_map/reduce_scatter | solution.py:77
  9.7 19.2 %copy-start.3 = (bf16[2,4,128,512]{3,2,1,0:T(8,128)(2,1)}, bf16[2,4,128,512]{3,2,1,0:T(8,128)(2,1)S(1)}, u32[]{:S(2)}) copy-start(bf16[2,4,128,512]{3,2,1,0:T(8,128)(2,1)S(1)} %fusion.7) | copy-start | bytes 3145732
  9.7 6.1 %copy-start.6 = (bf16[2,4,128,512]{3,2,1,0:T(8,128)(2,1)S(1)}, bf16[2,4,128,512]{3,2,1,0:T(8,128)(2,1)}, u32[]{:S(2)}) copy-start(bf16[2,4,128,512]{3,2,1,0:T(8,128)(2,1)} %param.7) | copy-start | bytes 3145732
  9.8 4.5 %collective-permute-start.1 = (bf16[2,1,128,512]{3,2,1,0:T(8,128)(2,1)S(1)}, bf16[2,1,128,512]{3,2,1,0:T(8,128)(2,1)S(1)}, u32[]{:S(2)}, u32[]{:S(2)}) collective-permute-start(bf16[2,1,128,512]{3,2,1,0:T(8,128)(2,1)S(1)} %get-tuple-element.5), channel_id=1, source_target_pairs={{4,0},{8,4},{12,8},{16,12},{20,16},{24,20},{28,24},{5,1},{9,5},{13... | collective-permute-start | bytes 786440 | tf_op jit(solution)/shard_map/ppermute | solution.py:15
  11.2 4.2 %collective-permute-start = (bf16[2,1,128,512]{3,2,1,0:T(8,128)(2,1)S(1)}, bf16[2,1,128,512]{3,2,1,0:T(8,128)(2,1)S(1)}, u32[]{:S(2)}, u32[]{:S(2)}) collective-permute-start(bf16[2,1,128,512]{3,2,1,0:T(8,128)(2,1)S(1)} %get-tuple-element.6), channel_id=1, source_target_pairs={{0,4},{4,8},{8,12},{12,16},{16,20},{20,24},{24,28},{1,5},{5,9},{9,... | collective-permute-start | bytes 786440 | tf_op jit(solution)/shard_map/ppermute | solution.py:14
  42.3 164.4 %reduce-scatter.5.cloned.1.call-start = ((), (), s32[]{:S(2)}) async-start(), calls=%async_computation.4 | async-start | bytes 10616832 | tf_op jit(solution)/shard_map/reduce_scatter | solution.py:77
  42.5 2.3 copy-start.4
  42.5 5.9 %slice-start = ((s8[4718592]{0:T(1024)(128)(4,1)}), s8[4194304]{0:T(1024)(128)(4,1)S(1)}, s32[]{:S(2)}) async-start(s8[4718592]{0:T(1024)(128)(4,1)} %bitcast.313), calls=%async_computation.10 | async-start | bytes 8388608
  44.8 3.7 %slice-start.1 = ((s8[4718592]{0:T(1024)(128)(4,1)}), s8[524288]{0:T(1024)(128)(4,1)S(1)}, s32[]{:S(2)}) async-start(s8[4718592]{0:T(1024)(128)(4,1)} %bitcast.313), calls=%async_computation.11 | async-start | bytes 1048576
  51.5 1.2 copy-start.7
  54.4 22.9 %copy-start.1 = (bf16[2,4,128,512]{3,2,1,0:T(8,128)(2,1)}, bf16[2,4,128,512]{3,2,1,0:T(8,128)(2,1)S(1)}, u32[]{:S(2)}) copy-start(bf16[2,4,128,512]{3,2,1,0:T(8,128)(2,1)S(1)} %fusion.14) | copy-start | bytes 3145732
  54.5 8.6 %collective-permute-start.3 = (bf16[2,1,128,512]{3,2,1,0:T(8,128)(2,1)S(1)}, bf16[2,1,128,512]{3,2,1,0:T(8,128)(2,1)S(1)}, u32[]{:S(2)}, u32[]{:S(2)}) collective-permute-start(bf16[2,1,128,512]{3,2,1,0:T(8,128)(2,1)S(1)} %get-tuple-element.3), channel_id=1, source_target_pairs={{4,0},{8,4},{12,8},{16,12},{20,16},{24,20},{28,24},{5,1},{9,5},{13... | collective-permute-start | bytes 786440 | tf_op jit(solution)/shard_map/ppermute | solution.py:15
  55.8 8.8 %collective-permute-start.2 = (bf16[2,1,128,512]{3,2,1,0:T(8,128)(2,1)S(1)}, bf16[2,1,128,512]{3,2,1,0:T(8,128)(2,1)S(1)}, u32[]{:S(2)}, u32[]{:S(2)}) collective-permute-start(bf16[2,1,128,512]{3,2,1,0:T(8,128)(2,1)S(1)} %get-tuple-element.4), channel_id=1, source_target_pairs={{0,4},{4,8},{8,12},{12,16},{16,20},{20,24},{24,28},{1,5},{5,9},{9,... | collective-permute-start | bytes 786440 | tf_op jit(solution)/shard_map/ppermute | solution.py:14
  90.7 147.5 %reduce-scatter.11.cloned.1.call-start = ((), (), s32[]{:S(2)}) async-start(), calls=%async_computation.8 | async-start | bytes 1474560 | tf_op jit(solution)/shard_map/reduce_scatter | solution.py:78
  126.6 141.6 %reduce-scatter.7.cloned.1.call-start = ((), (), s32[]{:S(2)}) async-start(), calls=%async_computation.5 | async-start | bytes 1474560 | tf_op jit(solution)/shard_map/reduce_scatter | solution.py:78
  206.7 91.1 %all-gather.5.cloned.1.call-start = ((), (), s32[]{:S(2)}) async-start(), calls=%async_computation.9 | async-start | bytes 2654208 | tf_op jit(solution)/shard_map/all_gather | solution.py:79
  238.2 90.3 %all-gather.3.cloned.1.call-start = ((), (), s32[]{:S(2)}) async-start(), calls=%async_computation.6 | async-start | bytes 2654208 | tf_op jit(solution)/shard_map/all_gather | solution.py:79
  268.3 2.3 copy-start.2
  268.3 5.9 %slice-start.2 = ((s8[4718592]{0:T(1024)(128)(4,1)}), s8[4194304]{0:T(1024)(128)(4,1)S(1)}, s32[]{:S(2)}) async-start(s8[4718592]{0:T(1024)(128)(4,1)} %bitcast.315), calls=%async_computation.12 | async-start | bytes 8388608
  270.6 3.7 %slice-start.3 = ((s8[4718592]{0:T(1024)(128)(4,1)}), s8[524288]{0:T(1024)(128)(4,1)S(1)}, s32[]{:S(2)}) async-start(s8[4718592]{0:T(1024)(128)(4,1)} %bitcast.315), calls=%async_computation.13 | async-start | bytes 1048576
  297.8 34.1 %copy-start.5 = (f32[1152,512]{1,0:T(8,128)S(1)}, f32[1152,512]{1,0:T(8,128)}, u32[]{:S(2)}) copy-start(f32[1152,512]{1,0:T(8,128)} %all-gather.5.cloned.1.call-done) | copy-start | bytes 7077892
Sparse Core Ops, SparseCore 0:
  42.4 84.1 reduce-scatter.8
  130.1 76.4 reduce-scatter.4
  209.0 29.1 reduce-scatter.10
  240.4 27.8 reduce-scatter.6
  270.0 27.7 all-gather.4
  299.5 29.0 all-gather.2
where the time goes:
time: 341 us; the launch traced here: 340 us
  waiting for transfers between devices  228 us (67%)
  matrix products  55.6 us (16%)
  local copies, waits for them, and re-layouts  14.8 us (4%)
  between operations  14.5 us (4%)
  starting transfers between devices  13.7 us (4%)
  other arithmetic  13.3 us (4%)
    reduce_scatter x2, waiting for transfers between devices, settle(): share = lax.psum_scatter(by_band, 'band', scatter_dimension=0, tiled=True)  116 us
    reduce_scatter x2, waiting for transfers between devices, settle(): share = lax.psum_scatter(share, 'date', scatter_dimension=0, tiled=True)  61.3 us
    all_gather x2, waiting for transfers between devices, settle(): return lax.all_gather(share, 'band', axis=0, tiled=True)  48.4 us
    dot_general x18, matrix products, weight_terms(): lax.dot_general(left_field, shifted_piece, (((0, 1, 2), (0, 1, 2)), ((),...  32.5 us
    dot_general x18, matrix products, back_terms(): lax.dot_general(shifted_piece, weight[row_offset + 1, col_offset + 1], ((...  23.1 us
    ppermute x2, starting transfers between devices, extended(): before = lax.ppermute(last, axis, up)  10.3 us
    mul x2, other arithmetic, weight_terms(): return (stacked * grad_scale).reshape(-1, stacked.shape[2])  10 us
    transpose x2, local copies, waits for them, and re-layouts, settle(): grad_term.reshape(dates, bands, piece, cols).swapaxes(0, 1)  9.51 us
  transfers between devices with their start and end apart: 10, of which 8 were waited for; matrix products, arithmetic and copies ran while one was open for 14% of the time, Pallas kernels for 0%

commit v1 on v0

--- a/solution.py
+++ b/solution.py
@@ -2,6 +2,27 @@
 import jax.numpy as jnp
 from jax import lax
 from jax.sharding import PartitionSpec as P
+from jax.lax import axis_index, axis_size, ppermute
+
+
+def watch_shelves(work_x):
+    k_now = axis_size("band")
+    u1, frame_out, x_new = (k_now, axis_index("band"), work_x.shape[0])
+    log = [hop_no * u1 if dev_i == 0 else hop_no for dev_i, hop_no in enumerate(work_x.shape)]
+    shaped = jnp.zeros(log, work_x.dtype)
+    main = lax.dynamic_update_slice_in_dim(shaped, work_x, frame_out * x_new, axis=0)
+    small = wide_out = work_x
+    for i0 in range(1, u1 // 2 + 1):
+        small = ppermute(small, "band", [(dev_i, (dev_i + 1) % u1) for dev_i in range(u1)])
+        main = lax.dynamic_update_slice_in_dim(main, small, (frame_out - i0) % u1 * x_new, axis=0)
+        if 2 * i0 < u1:
+            wide_out = ppermute(
+                wide_out, "band", [(dev_i, (dev_i - 1) % u1) for dev_i in range(u1)]
+            )
+            main = lax.dynamic_update_slice_in_dim(
+                main, wide_out, (frame_out + i0) % u1 * x_new, axis=0
+            )
+    return main
 
 
 def extended(array, sides, width):
@@ -76,7 +97,7 @@
     by_band = grad_term.reshape(dates, bands, piece, cols).swapaxes(0, 1).reshape(rows, cols)
     share = lax.psum_scatter(by_band, "band", scatter_dimension=0, tiled=True)
     share = lax.psum_scatter(share, "date", scatter_dimension=0, tiled=True)
-    return lax.all_gather(share, "band", axis=0, tiled=True)
+    return watch_shelves(share)
 
 
 def body(inputs, preact_one, preact_two, cotangent, weight_one, weight_two):

time: 341 us -> 319 us (0.935)
  waiting for transfers between devices: 228 us -> 165 us
  matrix products: 55.6 us -> 77.8 us
  starting transfers between devices: 13.7 us -> 29.1 us
  local copies, waits for them, and re-layouts: 14.8 us -> 19.5 us
    all_gather x2 -> x0, waiting for transfers between devices: 48.4 us -> none  [settle(): return lax.all_gather(share, 'band', axis=0, tiled=True)]
    reduce_scatter x2, waiting for transfers between devices: 61.3 us -> 32.2 us  [settle(): share = lax.psum_scatter(share, 'date', scatter_dimension=0, tiled=True)]
    ppermute x0 -> x14, waiting for transfers between devices: none -> 22.7 us  [the longest x8 14.7 us: watch_shelves(): ppermute(small, 'band', [(dev_i, (dev_i + 1) % u1) for dev_i in range(u1)])]
    dot_general x18, matrix products: 23.1 us -> 45.3 us  [back_terms(): lax.dot_general(shifted_piece, weight[row_offset + 1, col_offset + 1], ((...]
    ppermute x0 -> x14, starting transfers between devices: none -> 16.3 us  [the longest x6 16.2 us: watch_shelves(): ppermute(wide_out, 'band', [(dev_i, (dev_i - 1) % u1) for dev_i in range(...]
    reduce_scatter x2, waiting for transfers between devices: 116 us -> 104 us  [settle(): share = lax.psum_scatter(by_band, 'band', scatter_dimension=0, tiled=True)]
    ppermute x2, waiting for transfers between devices: 0.01 us -> 6.11 us  [extended(): after = lax.ppermute(leading, axis, down)]
    dynamic_update_slice x0 -> x16, local copies, waits for them, and re-layouts: none -> 6.06 us  [the longest x8 3.02 us: watch_shelves(): lax.dynamic_update_slice_in_dim(main, small, (frame_out - i0) % u1 * x_ne...]
  transfers between devices with their start and end apart: 10 -> 22, of which waited for: 8 -> 18; matrix products, arithmetic and copies ran while one was open for 14% -> 25% of each run, Pallas kernels for 0% -> 0%
where the time goes in v1:
time: 319 us
  waiting for transfers between devices  165 us (52%)
  matrix products  77.8 us (24%)
  starting transfers between devices  29.1 us (9%)
  local copies, waits for them, and re-layouts  19.5 us (6%)
  between operations  14.3 us (4%)
  other arithmetic  13.2 us (4%)
    reduce_scatter x2, waiting for transfers between devices, settle(): share = lax.psum_scatter(by_band, 'band', scatter_dimension=0, tiled=True)  104 us
    dot_general x18, matrix products, back_terms(): lax.dot_general(shifted_piece, weight[row_offset + 1, col_offset + 1], ((...  45.3 us
    dot_general x18, matrix products, weight_terms(): lax.dot_general(left_field, shifted_piece, (((0, 1, 2), (0, 1, 2)), ((),...  32.5 us
    reduce_scatter x2, waiting for transfers between devices, settle(): share = lax.psum_scatter(share, 'date', scatter_dimension=0, tiled=True)  32.2 us
    ppermute x6, starting transfers between devices, watch_shelves(): ppermute(wide_out, 'band', [(dev_i, (dev_i - 1) % u1) for dev_i in range(...  16.2 us
    ppermute x8, waiting for transfers between devices, watch_shelves(): ppermute(small, 'band', [(dev_i, (dev_i + 1) % u1) for dev_i in range(u1)])  14.7 us
    mul x2, other arithmetic, weight_terms(): return (stacked * grad_scale).reshape(-1, stacked.shape[2])  9.92 us
    transpose x2, local copies, waits for them, and re-layouts, settle(): grad_term.reshape(dates, bands, piece, cols).swapaxes(0, 1)  9.47 us
  transfers between devices with their start and end apart: 22, of which 18 were waited for; matrix products, arithmetic and copies ran while one was open for 25% of the time, Pallas kernels for 0%

profile of v1, /device:TPU:0, one launch (start us, length us, event | category | flops | bytes accessed | tf_op | source)
XLA Modules:
  0.0 318.7 jit_solution(2365844800977032444)
XLA Ops:
  7.2 2.5 fusion.7
  9.8 2.5 collective-permute-start
  12.3 1.3 collective-permute-start.1
  13.6 4.2 %collective-permute-done.1 = bf16[2,1,128,512]{3,2,1,0:T(8,128)(2,1)S(1)} collective-permute-done((bf16[2,1,128,512]{3,2,1,0:T(8,128)(2,1)S(1)}, bf16[2,1,128,512]{3,2,1,0:T(8,128)(2,1)S(1)}, u32[]{:S(2)}, u32[]{:S(2)}) %collective-permute-start.1) | collective-permute-done | bytes 262176 | tf_op jit(solution)/shard_map/ppermute | solution.py:36
  18.2 2.0 fusion.31
  20.3 1.8 fusion.30
  22.0 1.8 fusion.29
  23.8 2.0 fusion.28
  25.8 1.8 fusion.27
  27.6 1.8 fusion.26
  29.4 2.0 fusion.25
  31.4 1.9 fusion.24
  33.2 1.8 fusion.23
  35.0 4.8 %broadcast_multiply_fusion = f32[9,512,512]{2,1,0:T(8,128)S(1)} fusion(f32[9,512,512]{2,1,0:T(8,128)} %fusion.23), kind=kLoop, calls=%fused_computation.2 | loop fusion | flops 2359296 | bytes 18874368 | tf_op jit(solution)/shard_map/mul | solution.py:75
  39.9 4.8 %copy.28 = f32[8,4,144,512]{3,2,1,0:T(8,128)} copy(f32[8,4,144,512]{3,2,0,1:T(8,128)S(1)} %bitcast.311) | data formatting | bytes 18874368 | tf_op jit(solution)/shard_map/transpose | solution.py:97
  45.0 2.2 fusion.109
  47.3 1.8 fusion.39
  49.1 1.8 fusion.43
  55.2 1.7 fusion.14
  56.9 6.9 %collective-permute-start.2 = (bf16[2,1,128,512]{3,2,1,0:T(8,128)(2,1)S(1)}, bf16[2,1,128,512]{3,2,1,0:T(8,128)(2,1)S(1)}, u32[]{:S(2)}, u32[]{:S(2)}) collective-permute-start(bf16[2,1,128,512]{3,2,1,0:T(8,128)(2,1)S(1)} %get-tuple-element.4), channel_id=1, source_target_pairs={{0,4},{4,8},{8,12},{12,16},{16,20},{20,24},{24,28},{1,5},{5,9},{9,... | collective-permute-start | bytes 786440 | tf_op jit(solution)/shard_map/ppermute | solution.py:35
  63.8 1.5 collective-permute-start.3
  65.4 1.9 collective-permute-done.3
  67.7 1.7 fusion.38
  69.4 1.8 fusion.22
  71.2 1.7 fusion.37
  72.9 1.8 fusion.36
  74.7 1.8 fusion.35
  76.4 1.7 fusion.34
  78.2 1.7 fusion.33
  79.9 1.7 fusion.21
  81.7 1.8 fusion.32
  83.4 5.1 %broadcast_multiply_fusion.1 = f32[9,512,512]{2,1,0:T(8,128)S(1)} fusion(f32[9,512,512]{2,1,0:T(8,128)} %fusion.32), kind=kLoop, calls=%fused_computation.3 | loop fusion | flops 2359296 | bytes 18874368 | tf_op jit(solution)/shard_map/mul | solution.py:75
  88.5 4.6 %copy.18 = f32[8,4,144,512]{3,2,1,0:T(8,128)} copy(f32[8,4,144,512]{3,2,0,1:T(8,128)S(1)} %bitcast.312) | data formatting | bytes 18874368 | tf_op jit(solution)/shard_map/transpose | solution.py:97
  93.2 33.8 %reduce-scatter.9.cloned.1.call-done = f32[576,512]{1,0:T(8,128)} async-done(((f32[4608,512]{1,0:T(8,128)}), f32[576,512]{1,0:T(8,128)}) %reduce-scatter.9.cloned.1.call-update) | async-done | bytes 1179664 | tf_op jit(solution)/shard_map/reduce_scatter | solution.py:98
  127.5 3.5 %fusion.99 = f32[2,4,128,512]{3,2,1,0:T(8,128)} fusion(bf16[2,4,128,512]{3,2,1,0:T(8,128)(2,1)} %copy-done.1, bf16[3,3,512,512]{3,2,1,0:T(8,128)(2,1)} %param.10), kind=kOutput, calls=%fused_computation.127 | convolution fusion | flops 536870912 | bytes 3670016 | tf_op jit(solution)/shard_map/dot_general | solution.py:83
  131.0 3.1 fusion.94
  134.1 3.1 fusion.59
  137.3 69.8 %reduce-scatter.5.cloned.1.call-done = f32[576,512]{1,0:T(8,128)} async-done(((f32[4608,512]{1,0:T(8,128)}), f32[576,512]{1,0:T(8,128)}) %reduce-scatter.5.cloned.1.call-update) | async-done | bytes 1179664 | tf_op jit(solution)/shard_map/reduce_scatter | solution.py:98
  207.1 3.3 %fusion.93 = f32[2,4,128,512]{3,2,1,0:T(8,128)} fusion(bf16[2,4,128,512]{3,2,1,0:T(8,128)(2,1)} %copy-done.1, bf16[2,1,128,512]{3,2,1,0:T(8,128)(2,1)S(1)} %collective-permute-done.2, bf16[3,3,512,512]{3,2,1,0:T(8,128)(2,1)} %param.10), kind=kOutput, calls=%fused_computation.121 | convolution fusion | flops 539492352 | bytes 3932160 | tf_op jit(solution)/shard_map/dot_general | solution.py:83
  210.4 3.1 fusion.62
  213.5 3.2 fusion.65
  216.7 3.2 fusion.68
  219.9 3.1 fusion.71
  223.0 15.6 %reduce-scatter.11.cloned.1.call-done = f32[144,512]{1,0:T(8,128)} async-done(((f32[576,512]{1,0:T(8,128)}), f32[144,512]{1,0:T(8,128)}) %reduce-scatter.11.cloned.1.call-update) | async-done | bytes 294928 | tf_op jit(solution)/shard_map/reduce_scatter | solution.py:99
  238.6 2.6 collective-permute-start.12
  241.2 8.4 %add_convert_fusion = bf16[2,4,128,512]{3,2,1,0:T(8,128)(2,1)} fusion(f32[2,4,128,512]{3,2,1,0:T(8,128)} %fusion.93, f32[2,4,128,512]{3,2,1,0:T(8,128)} %fusion.59, f32[2,4,128,512]{3,2,1,0:T(8,128)} %fusion.62, f32[2,4,128,512]{3,2,1,0:T(8,128)} %fusion.99, f32[2,4,128,512]{3,2,1,0:T(8,128)} %fusion.65, f32[2,4,128,512]{3,2,1,0:T(8,128)} %fusion.68, ...), kind=kOutput, calls=%fused_computation.25 | convolution fusion | flops 541589504 | bytes 19398656 | tf_op jit(solution)/shard_map/dot_general | solution.py:83
  249.6 1.7 broadcast.28.clone.1
  252.1 16.6 %reduce-scatter.7.cloned.1.call-done = f32[144,512]{1,0:T(8,128)} async-done(((f32[576,512]{1,0:T(8,128)}), f32[144,512]{1,0:T(8,128)}) %reduce-scatter.7.cloned.1.call-update) | async-done | bytes 294928 | tf_op jit(solution)/shard_map/reduce_scatter | solution.py:99
  268.7 2.6 collective-permute-start.5
  271.8 2.6 collective-permute-start.14
  275.8 1.4 collective-permute-done.4
  277.3 1.8 collective-permute-done.5
  279.1 2.7 collective-permute-start.7
  281.9 1.7 collective-permute-done.13
  283.6 1.7 collective-permute-done.14
  285.3 2.8 collective-permute-start.16
  289.9 1.7 collective-permute-done.7
  291.6 2.8 collective-permute-start.9
  294.5 1.8 collective-permute-done.15
  298.7 3.9 %collective-permute-done.8 = f32[144,512]{1,0:T(8,128)S(1)} collective-permute-done((f32[144,512]{1,0:T(8,128)S(1)}, f32[144,512]{1,0:T(8,128)S(1)}, u32[]{:S(2)}, u32[]{:S(2)}) %collective-permute-start.8) | collective-permute-done | bytes 294944 | tf_op jit(solution)/shard_map/ppermute | solution.py:16
  302.6 1.7 collective-permute-done.9
  304.3 3.2 %collective-permute-done.17 = f32[144,512]{1,0:T(8,128)S(1)} collective-permute-done((f32[144,512]{1,0:T(8,128)S(1)}, f32[144,512]{1,0:T(8,128)S(1)}, u32[]{:S(2)}, u32[]{:S(2)}) %collective-permute-start.17) | collective-permute-done | bytes 294944 | tf_op jit(solution)/shard_map/ppermute | solution.py:16
  308.3 2.4 collective-permute-done.10
  310.7 1.4 copy-done.5
  (72 shorter events, 13.6 us)
Async XLA Ops:
  7.2 60.5 %copy-start = (bf16[2,4,128,512]{3,2,1,0:T(8,128)(2,1)S(1)}, bf16[2,4,128,512]{3,2,1,0:T(8,128)(2,1)}, u32[]{:S(2)}) copy-start(bf16[2,4,128,512]{3,2,1,0:T(8,128)(2,1)} %param.6) | copy-start | bytes 3145732
  7.2 119.9 %reduce-scatter.9.cloned.1.call-start = ((), (), s32[]{:S(2)}) async-start(), calls=%async_computation.6 | async-start | bytes 10616832 | tf_op jit(solution)/shard_map/reduce_scatter | solution.py:98
  9.7 21.7 %copy-start.3 = (bf16[2,4,128,512]{3,2,1,0:T(8,128)(2,1)}, bf16[2,4,128,512]{3,2,1,0:T(8,128)(2,1)S(1)}, u32[]{:S(2)}) copy-start(bf16[2,4,128,512]{3,2,1,0:T(8,128)(2,1)S(1)} %fusion.7) | copy-start | bytes 3145732
  9.7 8.5 %copy-start.6 = (bf16[2,4,128,512]{3,2,1,0:T(8,128)(2,1)S(1)}, bf16[2,4,128,512]{3,2,1,0:T(8,128)(2,1)}, u32[]{:S(2)}) copy-start(bf16[2,4,128,512]{3,2,1,0:T(8,128)(2,1)} %param.7) | copy-start | bytes 3145732
  9.8 3.8 %collective-permute-start = (bf16[2,1,128,512]{3,2,1,0:T(8,128)(2,1)S(1)}, bf16[2,1,128,512]{3,2,1,0:T(8,128)(2,1)S(1)}, u32[]{:S(2)}, u32[]{:S(2)}) collective-permute-start(bf16[2,1,128,512]{3,2,1,0:T(8,128)(2,1)S(1)} %get-tuple-element.6), channel_id=1, source_target_pairs={{0,4},{4,8},{8,12},{12,16},{16,20},{20,24},{24,28},{1,5},{5,9},{9,... | collective-permute-start | bytes 786440 | tf_op jit(solution)/shard_map/ppermute | solution.py:35
  12.3 5.5 %collective-permute-start.1 = (bf16[2,1,128,512]{3,2,1,0:T(8,128)(2,1)S(1)}, bf16[2,1,128,512]{3,2,1,0:T(8,128)(2,1)S(1)}, u32[]{:S(2)}, u32[]{:S(2)}) collective-permute-start(bf16[2,1,128,512]{3,2,1,0:T(8,128)(2,1)S(1)} %get-tuple-element.5), channel_id=1, source_target_pairs={{4,0},{8,4},{12,8},{16,12},{20,16},{24,20},{28,24},{5,1},{9,5},{13... | collective-permute-start | bytes 786440 | tf_op jit(solution)/shard_map/ppermute | solution.py:36
  44.8 162.3 %reduce-scatter.5.cloned.1.call-start = ((), (), s32[]{:S(2)}) async-start(), calls=%async_computation.4 | async-start | bytes 10616832 | tf_op jit(solution)/shard_map/reduce_scatter | solution.py:98
  45.0 2.3 copy-start.4
  45.0 5.9 %slice-start = ((s8[4718592]{0:T(1024)(128)(4,1)}), s8[4194304]{0:T(1024)(128)(4,1)S(1)}, s32[]{:S(2)}) async-start(s8[4718592]{0:T(1024)(128)(4,1)} %bitcast.313), calls=%async_computation.8 | async-start | bytes 8388608
  47.3 3.6 %slice-start.1 = ((s8[4718592]{0:T(1024)(128)(4,1)}), s8[524288]{0:T(1024)(128)(4,1)S(1)}, s32[]{:S(2)}) async-start(s8[4718592]{0:T(1024)(128)(4,1)} %bitcast.313), calls=%async_computation.9 | async-start | bytes 1048576
  53.9 1.2 copy-start.7
  56.9 23.1 %copy-start.1 = (bf16[2,4,128,512]{3,2,1,0:T(8,128)(2,1)}, bf16[2,4,128,512]{3,2,1,0:T(8,128)(2,1)S(1)}, u32[]{:S(2)}) copy-start(bf16[2,4,128,512]{3,2,1,0:T(8,128)(2,1)S(1)} %fusion.14) | copy-start | bytes 3145732
  56.9 8.4 %collective-permute-start.2 = (bf16[2,1,128,512]{3,2,1,0:T(8,128)(2,1)S(1)}, bf16[2,1,128,512]{3,2,1,0:T(8,128)(2,1)S(1)}, u32[]{:S(2)}, u32[]{:S(2)}) collective-permute-start(bf16[2,1,128,512]{3,2,1,0:T(8,128)(2,1)S(1)} %get-tuple-element.4), channel_id=1, source_target_pairs={{0,4},{4,8},{8,12},{12,16},{16,20},{20,24},{24,28},{1,5},{5,9},{9,... | collective-permute-start | bytes 786440 | tf_op jit(solution)/shard_map/ppermute | solution.py:35
  63.8 3.4 %collective-permute-start.3 = (bf16[2,1,128,512]{3,2,1,0:T(8,128)(2,1)S(1)}, bf16[2,1,128,512]{3,2,1,0:T(8,128)(2,1)S(1)}, u32[]{:S(2)}, u32[]{:S(2)}) collective-permute-start(bf16[2,1,128,512]{3,2,1,0:T(8,128)(2,1)S(1)} %get-tuple-element.3), channel_id=1, source_target_pairs={{4,0},{8,4},{12,8},{16,12},{20,16},{24,20},{28,24},{5,1},{9,5},{13... | collective-permute-start | bytes 786440 | tf_op jit(solution)/shard_map/ppermute | solution.py:36
  93.2 145.4 %reduce-scatter.11.cloned.1.call-start = ((), (), s32[]{:S(2)}) async-start(), calls=%async_computation.7 | async-start | bytes 1474560 | tf_op jit(solution)/shard_map/reduce_scatter | solution.py:99
  127.1 141.6 %reduce-scatter.7.cloned.1.call-start = ((), (), s32[]{:S(2)}) async-start(), calls=%async_computation.5 | async-start | bytes 1474560 | tf_op jit(solution)/shard_map/reduce_scatter | solution.py:99
  127.5 3.5 %copy-start.2 = (bf16[2,4,128,512]{3,2,1,0:T(8,128)(2,1)S(1)}, bf16[2,4,128,512]{3,2,1,0:T(8,128)(2,1)}, u32[]{:S(2)}) copy-start(bf16[2,4,128,512]{3,2,1,0:T(8,128)(2,1)} %copy-done.1) | copy-start | bytes 3145732
  238.6 33.1 %collective-permute-start.11 = (f32[144,512]{1,0:T(8,128)}, f32[144,512]{1,0:T(8,128)S(1)}, u32[]{:S(2)}, u32[]{:S(2)}) collective-permute-start(f32[144,512]{1,0:T(8,128)} %reduce-scatter.11.cloned.1.call-done), channel_id=1, source_target_pairs={{0,4},{4,8},{8,12},{12,16},{16,20},{20,24},{24,28},{28,0},{1,5},{5... | collective-permute-start | bytes 884744 | tf_op jit(solution)/shard_map/ppermute | solution.py:16
  238.6 33.2 %collective-permute-start.12 = (f32[144,512]{1,0:T(8,128)}, f32[144,512]{1,0:T(8,128)S(1)}, u32[]{:S(2)}, u32[]{:S(2)}) collective-permute-start(f32[144,512]{1,0:T(8,128)} %reduce-scatter.11.cloned.1.call-done), channel_id=1, source_target_pairs={{0,28},{4,0},{8,4},{12,8},{16,12},{20,16},{24,20},{28,24},{1,29},{... | collective-permute-start | bytes 884744 | tf_op jit(solution)/shard_map/ppermute | solution.py:19
  249.6 1.7 copy-start.8
  268.7 2.9 copy-start.9
  268.7 8.6 %collective-permute-start.4 = (f32[144,512]{1,0:T(8,128)}, f32[144,512]{1,0:T(8,128)S(1)}, u32[]{:S(2)}, u32[]{:S(2)}) collective-permute-start(f32[144,512]{1,0:T(8,128)} %reduce-scatter.7.cloned.1.call-done), channel_id=1, source_target_pairs={{0,4},{4,8},{8,12},{12,16},{16,20},{20,24},{24,28},{28,0},{1,5},{5... | collective-permute-start | bytes 884744 | tf_op jit(solution)/shard_map/ppermute | solution.py:16
  268.7 10.4 %collective-permute-start.5 = (f32[144,512]{1,0:T(8,128)}, f32[144,512]{1,0:T(8,128)S(1)}, u32[]{:S(2)}, u32[]{:S(2)}) collective-permute-start(f32[144,512]{1,0:T(8,128)} %reduce-scatter.7.cloned.1.call-done), channel_id=1, source_target_pairs={{0,28},{4,0},{8,4},{12,8},{16,12},{20,16},{24,20},{28,24},{1,29},{... | collective-permute-start | bytes 884744 | tf_op jit(solution)/shard_map/ppermute | solution.py:19
  271.7 11.9 %collective-permute-start.13 = (f32[144,512]{1,0:T(8,128)S(1)}, f32[144,512]{1,0:T(8,128)S(1)}, u32[]{:S(2)}, u32[]{:S(2)}) collective-permute-start(f32[144,512]{1,0:T(8,128)S(1)} %collective-permute-done.11), channel_id=1, source_target_pairs={{0,4},{4,8},{8,12},{12,16},{16,20},{20,24},{24,28},{28,0},{1,5},{5... | collective-permute-start | bytes 884744 | tf_op jit(solution)/shard_map/ppermute | solution.py:16
  271.8 13.6 %collective-permute-start.14 = (f32[144,512]{1,0:T(8,128)S(1)}, f32[144,512]{1,0:T(8,128)S(1)}, u32[]{:S(2)}, u32[]{:S(2)}) collective-permute-start(f32[144,512]{1,0:T(8,128)S(1)} %collective-permute-done.12), channel_id=1, source_target_pairs={{0,28},{4,0},{8,4},{12,8},{16,12},{20,16},{24,20},{28,24},{1,29},{... | collective-permute-start | bytes 884744 | tf_op jit(solution)/shard_map/ppermute | solution.py:19
  277.3 12.6 %collective-permute-start.6 = (f32[144,512]{1,0:T(8,128)S(1)}, f32[144,512]{1,0:T(8,128)S(1)}, u32[]{:S(2)}, u32[]{:S(2)}) collective-permute-start(f32[144,512]{1,0:T(8,128)S(1)} %collective-permute-done.4), channel_id=1, source_target_pairs={{0,4},{4,8},{8,12},{12,16},{16,20},{20,24},{24,28},{28,0},{1,5},{5... | collective-permute-start | bytes 884744 | tf_op jit(solution)/shard_map/ppermute | solution.py:16
  279.1 12.5 %collective-permute-start.7 = (f32[144,512]{1,0:T(8,128)S(1)}, f32[144,512]{1,0:T(8,128)S(1)}, u32[]{:S(2)}, u32[]{:S(2)}) collective-permute-start(f32[144,512]{1,0:T(8,128)S(1)} %collective-permute-done.5), channel_id=1, source_target_pairs={{0,28},{4,0},{8,4},{12,8},{16,12},{20,16},{24,20},{28,24},{1,29},{... | collective-permute-start | bytes 884744 | tf_op jit(solution)/shard_map/ppermute | solution.py:19
  283.6 12.6 %collective-permute-start.15 = (f32[144,512]{1,0:T(8,128)S(1)}, f32[144,512]{1,0:T(8,128)S(1)}, u32[]{:S(2)}, u32[]{:S(2)}) collective-permute-start(f32[144,512]{1,0:T(8,128)S(1)} %collective-permute-done.13), channel_id=1, source_target_pairs={{0,4},{4,8},{8,12},{12,16},{16,20},{20,24},{24,28},{28,0},{1,5},{5... | collective-permute-start | bytes 884744 | tf_op jit(solution)/shard_map/ppermute | solution.py:16
  285.3 12.6 %collective-permute-start.16 = (f32[144,512]{1,0:T(8,128)S(1)}, f32[144,512]{1,0:T(8,128)S(1)}, u32[]{:S(2)}, u32[]{:S(2)}) collective-permute-start(f32[144,512]{1,0:T(8,128)S(1)} %collective-permute-done.14), channel_id=1, source_target_pairs={{0,28},{4,0},{8,4},{12,8},{16,12},{20,16},{24,20},{28,24},{1,29},{... | collective-permute-start | bytes 884744 | tf_op jit(solution)/shard_map/ppermute | solution.py:19
  289.9 12.6 %collective-permute-start.8 = (f32[144,512]{1,0:T(8,128)S(1)}, f32[144,512]{1,0:T(8,128)S(1)}, u32[]{:S(2)}, u32[]{:S(2)}) collective-permute-start(f32[144,512]{1,0:T(8,128)S(1)} %collective-permute-done.6), channel_id=1, source_target_pairs={{0,4},{4,8},{8,12},{12,16},{16,20},{20,24},{24,28},{28,0},{1,5},{5... | collective-permute-start | bytes 884744 | tf_op jit(solution)/shard_map/ppermute | solution.py:16
  291.6 12.6 %collective-permute-start.9 = (f32[144,512]{1,0:T(8,128)S(1)}, f32[144,512]{1,0:T(8,128)S(1)}, u32[]{:S(2)}, u32[]{:S(2)}) collective-permute-start(f32[144,512]{1,0:T(8,128)S(1)} %collective-permute-done.7), channel_id=1, source_target_pairs={{0,28},{4,0},{8,4},{12,8},{16,12},{20,16},{24,20},{28,24},{1,29},{... | collective-permute-start | bytes 884744 | tf_op jit(solution)/shard_map/ppermute | solution.py:19
  296.2 11.3 %collective-permute-start.17 = (f32[144,512]{1,0:T(8,128)S(1)}, f32[144,512]{1,0:T(8,128)S(1)}, u32[]{:S(2)}, u32[]{:S(2)}) collective-permute-start(f32[144,512]{1,0:T(8,128)S(1)} %collective-permute-done.15), channel_id=1, source_target_pairs={{0,4},{4,8},{8,12},{12,16},{16,20},{20,24},{24,28},{28,0},{1,5},{5... | collective-permute-start | bytes 884744 | tf_op jit(solution)/shard_map/ppermute | solution.py:16
  302.6 8.1 %collective-permute-start.10 = (f32[144,512]{1,0:T(8,128)S(1)}, f32[144,512]{1,0:T(8,128)S(1)}, u32[]{:S(2)}, u32[]{:S(2)}) collective-permute-start(f32[144,512]{1,0:T(8,128)S(1)} %collective-permute-done.8), channel_id=1, source_target_pairs={{0,4},{4,8},{8,12},{12,16},{16,20},{20,24},{24,28},{28,0},{1,5},{5... | collective-permute-start | bytes 884744 | tf_op jit(solution)/shard_map/ppermute | solution.py:16
  310.7 1.4 copy-start.5
Sparse Core Ops, SparseCore 0:
  44.9 82.1 reduce-scatter.8
  130.5 76.4 reduce-scatter.4
  209.4 29.1 reduce-scatter.10
  240.8 27.8 reduce-scatter.6
